TPU v7x, 256 devices: a whole 4x4x8 slice. The times are simulated.
256 devices in a mesh: gx: 16 (over x, z_hi, core), gy: 4 (over z_lo), gz: 4 (over y).
Axes of the slice: x: 4, y: 4, z: 8 (z_hi: 2, z_lo: 4; z = z_hi * 4 + z_lo), core: 2. Of those that a mesh axis runs over, the one named last changes fastest.
Arguments:
- image_slab: float32 [64, 1024, 1024], P(('gz', 'gx'), None, 'gy'), may hold values from -6 to 6
- deformed_slab: float32 [64, 1024, 1024], P(('gz', 'gx'), None, 'gy'), may hold values from -6 to 6
- shifts: int32 [2, 3, 4, 16, 4], P(None, None, 'gz', 'gx', 'gy'), may hold values from -8 to 8, as said below
Outputs:
- displacement: float32 [3, 12, 144, 132], P(None, 'gz', 'gx', 'gy')
- residual_map: float32 [64, 1024, 1024], P('gz', 'gx', 'gy')
Inputs may be any that keep to these rules, and one draw needn't show every extreme that they name: `shifts`: every component lies within -8 to 8, and both ends are taken by some entry.
All inputs are finite; a program needn't handle non-finite values.
Results may differ from a plain program's by a relative error of at most 0.0003.
Values sent between devices are 32-bit elements; how exact they have to be, the bound alone decides.
No kernel may reach another device: no remote copies, remote signals or barrier semaphores. Data moves between devices by JAX's collectives and lax.ppermute only.
A program may use at most 128 MiB of HBM per device.

v0:
```python
import numpy as np
import jax
import jax.numpy as jnp
from jax import lax
from jax.sharding import PartitionSpec as P

ELEMENT = 8
DMAX = 8
ITERS = 2
SWEEPS = 3
DAMPING = 0.7
REGULARIZE = 4.0
HI = lax.Precision.HIGHEST


def shape_table(voxel_count, squared=False):
    voxel = np.arange(voxel_count)
    fraction = ((voxel % ELEMENT).astype(np.float32) + 0.5) / ELEMENT
    owning = voxel // ELEMENT
    nodes = np.arange(voxel_count // ELEMENT + 1)
    lower = (nodes[None, :] == owning[:, None]) * (1.0 - fraction)[:, None]
    upper = (nodes[None, :] == owning[:, None] + 1) * fraction[:, None]
    table = (lower + upper).astype(np.float32)
    if squared:
        table = table * table
    return jnp.asarray(table)


def z_weights(squared=False):
    fraction = (np.arange(ELEMENT, dtype=np.float32) + 0.5) / ELEMENT
    lower = 1.0 - fraction
    if squared:
        return (lower * lower, fraction * fraction)
    return (lower, fraction)


def neighbours(axis):
    count = lax.axis_size(axis)
    forward = [(i, i + 1) for i in range(count - 1)]
    backward = [(i + 1, i) for i in range(count - 1)]
    return (forward, backward)


def halo(block, axis, dim, width):
    forward, backward = neighbours(axis)
    size = block.shape[dim]
    low = lax.ppermute(lax.slice_in_dim(block, size - width, size, axis=dim), axis, forward)
    high = lax.ppermute(lax.slice_in_dim(block, 0, width, axis=dim), axis, backward)
    return jnp.concatenate([low, block, high], axis=dim)


def share(partial_value):
    value = partial_value
    for axis, dim in (("gz", 1), ("gx", 2), ("gy", 3)):
        forward, backward = neighbours(axis)
        size = value.shape[dim]
        first = lax.slice_in_dim(value, 0, 1, axis=dim)
        last = lax.slice_in_dim(value, size - 1, size, axis=dim)
        from_low = lax.ppermute(last, axis, forward)
        from_high = lax.ppermute(first, axis, backward)
        middle = lax.slice_in_dim(value, 1, size - 1, axis=dim)
        value = jnp.concatenate([first + from_low, middle, last + from_high], axis=dim)
    return value


def cut_range(array, axis, start, length):
    return lax.slice_in_dim(array, start, start + length, axis=axis)


def smooth(array, axis):
    length = array.shape[axis] - 2
    return (
        cut_range(array, axis, 0, length)
        + 2.0 * cut_range(array, axis, 1, length)
        + cut_range(array, axis, 2, length)
    ) * 0.25


def differ(array, axis):
    length = array.shape[axis] - 2
    return (cut_range(array, axis, 2, length) - cut_range(array, axis, 0, length)) * 0.5


def gradients(extended):
    along_z = smooth(smooth(differ(extended, 0), 1), 2)
    along_x = smooth(smooth(differ(extended, 1), 0), 2)
    along_y = smooth(smooth(differ(extended, 2), 0), 1)
    return jnp.stack([along_z, along_x, along_y])


def interp_xy(nodal, table_x, table_y):
    step = jnp.einsum("cabd,yd->caby", nodal, table_y, precision=HI)
    return jnp.einsum("caby,xb->caxy", step, table_x, precision=HI)


def expand_z(values, weights):
    lower, upper = weights
    count = values.shape[1] - 1
    low = values[:, :count, None]
    high = values[:, 1:, None]
    shape = (1, 1, ELEMENT, 1, 1)
    joined = low * lower.reshape(shape) + high * upper.reshape(shape)
    return joined.reshape((values.shape[0], count * ELEMENT) + values.shape[2:])


def interpolate(nodal, tables, weights):
    return expand_z(interp_xy(nodal, *tables), weights)


def reduce_z(field, weights):
    lower, upper = weights
    count = field.shape[1] // ELEMENT
    blocks = field.reshape((field.shape[0], count, ELEMENT) + field.shape[2:])
    shape = (1, 1, ELEMENT, 1, 1)
    low = jnp.sum(blocks * lower.reshape(shape), axis=2)
    high = jnp.sum(blocks * upper.reshape(shape), axis=2)
    parts = [low[:, :1]]
    for e in range(1, count):
        parts.append(high[:, e - 1 : e] + low[:, e : e + 1])
    parts.append(high[:, count - 1 :])
    return jnp.concatenate(parts, axis=1)


def restrict(field, tables, weights):
    table_x, table_y = tables
    step = reduce_z(field, weights)
    step = jnp.einsum("caxy,xb->caby", step, table_x, precision=HI)
    return jnp.einsum("caby,yd->cabd", step, table_y, precision=HI)


def invert(diag):
    a, b, c, d, e, f = (diag[0], diag[1], diag[2], diag[3], diag[4], diag[5])
    i00 = b * c - f * f
    i11 = a * c - e * e
    i22 = a * b - d * d
    i01 = e * f - d * c
    i02 = d * f - b * e
    i12 = d * e - a * f
    det = a * i00 + d * i01 + e * i02
    return jnp.stack([i00, i11, i22, i01, i02, i12]) / det


def apply_inverse(inverse, vector):
    out_z = inverse[0] * vector[0] + inverse[3] * vector[1] + inverse[4] * vector[2]
    out_x = inverse[3] * vector[0] + inverse[1] * vector[1] + inverse[5] * vector[2]
    out_y = inverse[4] * vector[0] + inverse[5] * vector[1] + inverse[2] * vector[2]
    return jnp.stack([out_z, out_x, out_y])


def bricks_of(image_slab, deformed_slab):
    image = lax.all_to_all(image_slab, "gx", split_axis=1, concat_axis=0, tiled=True)
    deformed = lax.all_to_all(deformed_slab, "gx", split_axis=1, concat_axis=0, tiled=True)
    both = jnp.stack([image, deformed])
    both = halo(both, "gy", 3, DMAX)
    both = halo(both, "gx", 2, DMAX)
    forward, backward = neighbours("gz")
    bz, nx, ny = both.shape[1:]
    image = both[0]
    deformed = both[1]
    to_high = jnp.concatenate([deformed[bz - DMAX :], image[bz - 1 :]], axis=0)
    to_low = jnp.concatenate([deformed[:DMAX], image[:1]], axis=0)
    from_low = lax.ppermute(to_high, "gz", forward)
    from_high = lax.ppermute(to_low, "gz", backward)
    deformed_ext = jnp.concatenate([from_low[:DMAX], deformed, from_high[:DMAX]], axis=0)
    image_ext = jnp.concatenate([from_low[DMAX:], image, from_high[DMAX:]], axis=0)
    image_ext = image_ext[:, DMAX - 1 : nx - DMAX + 1, DMAX - 1 : ny - DMAX + 1]
    return (image_ext, deformed_ext)


def shards(image_slab, deformed_slab, shifts):
    image_ext, deformed_ext = bricks_of(image_slab, deformed_slab)
    image = image_ext[1:-1, 1:-1, 1:-1]
    z_count, x_count, y_count = image.shape
    grads = gradients(image_ext)
    tables = (shape_table(x_count), shape_table(y_count))
    tables_sq = (shape_table(x_count, True), shape_table(y_count, True))
    weights = z_weights(False)
    weights_sq = z_weights(True)
    pairs = ((0, 0), (1, 1), (2, 2), (0, 1), (0, 2), (1, 2))

    def residual(moved, warped_now, offset):
        offset_float = offset.astype(jnp.float32)[:, None, None, None]
        return image - warped_now - jnp.sum(grads * (moved - offset_float), axis=0)

    def warp(iteration):
        offset = shifts[iteration, :, 0, 0, 0]
        starts = [DMAX + offset[0], DMAX + offset[1], DMAX + offset[2]]
        return (lax.dynamic_slice(deformed_ext, starts, (z_count, x_count, y_count)), offset)

    def operator(delta):
        inner = jnp.sum(grads * interpolate(delta, tables, weights), axis=0)
        return share(restrict(grads * inner[None], tables, weights))

    warped, offset = warp(0)
    resid = (
        image - warped + jnp.sum(grads * offset.astype(jnp.float32)[:, None, None, None], axis=0)
    )
    products = jnp.stack([grads[i] * grads[j] for i, j in pairs])
    first = jnp.concatenate(
        [restrict(products, tables_sq, weights_sq), restrict(grads * resid[None], tables, weights)],
        axis=0,
    )
    first = share(first)
    diag = (
        first[:6]
        + REGULARIZE * jnp.array([1.0, 1.0, 1.0, 0.0, 0.0, 0.0], jnp.float32)[:, None, None, None]
    )
    inverse = invert(diag)
    rhs = first[6:]
    nodal = jnp.zeros(
        (3, z_count // ELEMENT + 1, x_count // ELEMENT + 1, y_count // ELEMENT + 1), jnp.float32
    )
    for iteration in range(ITERS):
        if iteration > 0:
            warped, offset = warp(iteration)
            resid = residual(interpolate(nodal, tables, weights), warped, offset)
            rhs = share(restrict(grads * resid[None], tables, weights))
        delta = DAMPING * apply_inverse(inverse, rhs)
        for sweep in range(SWEEPS - 1):
            applied = operator(delta) + REGULARIZE * delta
            delta = delta + DAMPING * apply_inverse(inverse, rhs - applied)
        nodal = nodal + delta
    final = residual(interpolate(nodal, tables, weights), warped, offset)
    return (nodal, final)


def solution(mesh):
    return jax.shard_map(
        shards,
        mesh=mesh,
        in_specs=(
            P(("gz", "gx"), None, "gy"),
            P(("gz", "gx"), None, "gy"),
            P(None, None, "gz", "gx", "gy"),
        ),
        out_specs=(P(None, "gz", "gx", "gy"), P("gz", "gx", "gy")),
        check_vma=False,
    )
```

profile of v0, /device:TPU:4, one launch (start us, length us, event | category | flops | bytes accessed | tf_op | source)
XLA Modules:
  0.0 536.1 jit_solution(17858841931184547508)
XLA Ops:
  0.6 3.4 copy.56
  4.0 11.4 %all-to-all-start.1 = ((f32[1,1024,256]{2,0,1:T(1,128)}), f32[1,1024,256]{2,0,1:T(1,128)S(1)}, u32[]{:S(2)}, u32[]{:S(2)}) async-start(f32[1,1024,256]{2,0,1:T(1,128)} %copy.56), calls=%async_computation.1 | async-start | bytes 2097152 | tf_op jit(solution)/shard_map/all_to_all | solution.py:152
  17.5 18.0 %all-to-all-done.1 = f32[1,1024,256]{2,0,1:T(1,128)S(1)} async-done(((f32[1,1024,256]{2,0,1:T(1,128)}), f32[1,1024,256]{2,0,1:T(1,128)S(1)}, u32[]{:S(2)}, u32[]{:S(2)}) %all-to-all-start.1) | async-done | bytes 1048608 | tf_op jit(solution)/shard_map/all_to_all | solution.py:152
  35.6 6.8 %all-to-all-start = ((f32[1,1024,256]{2,0,1:T(1,128)}), f32[1,1024,256]{2,0,1:T(1,128)}, u32[]{:S(2)}, u32[]{:S(2)}) async-start(f32[1,1024,256]{2,0,1:T(1,128)} %copy.55), calls=%async_computation | async-start | bytes 2097152 | tf_op jit(solution)/shard_map/all_to_all | solution.py:151
  43.3 17.1 %all-to-all-done = f32[1,1024,256]{2,0,1:T(1,128)} async-done(((f32[1,1024,256]{2,0,1:T(1,128)}), f32[1,1024,256]{2,0,1:T(1,128)}, u32[]{:S(2)}, u32[]{:S(2)}) %all-to-all-start) | async-done | bytes 1048608 | tf_op jit(solution)/shard_map/all_to_all | solution.py:151
  60.4 3.9 copy.57
  66.7 15.6 %collective-permute-start = (f32[2,16,64,8]{2,3,1,0:T(8,128)S(1)}, f32[2,16,64,8]{2,3,1,0:T(8,128)S(1)}, u32[]{:S(2)}, u32[]{:S(2)}) collective-permute-start(f32[2,16,64,8]{2,3,1,0:T(8,128)S(1)} %get-tuple-element.59), channel_id=1, source_target_pairs={{0,4},{4,8},{8,12},{1,5},{5,9},{9,13},{2,6},{6,10},{10,14},{3,7},{... | collective-permute-start | bytes 196616 | tf_op jit(solution)/shard_map/ppermute | solution.py:47
  85.6 5.0 fusion.117
  90.6 3.3 copy.60
  95.8 4.0 copy.59
  99.8 2.4 collective-permute-start.2
  102.2 2.9 copy.62
  105.1 13.0 %collective-permute-done.2 = f32[2,16,8,272]{3,2,1,0:T(8,128)} collective-permute-done((f32[2,16,8,272]{3,2,1,0:T(8,128)}, f32[2,16,8,272]{3,2,1,0:T(8,128)}, u32[]{:S(2)}, u32[]{:S(2)}) %collective-permute-start.2) | collective-permute-done | bytes 278560 | tf_op jit(solution)/shard_map/ppermute | solution.py:47
  118.0 3.8 copy.61
  121.8 6.1 %pad_maximum_fusion.2 = f32[2,16,80,272]{2,3,1,0:T(8,128)S(1)} fusion(f32[2,16,8,272]{2,3,1,0:T(8,128)} %copy.62, f32[2,16,64,8]{2,3,1,0:T(8,128)S(1)} %collective-permute-done.1, f32[1,16,64,256]{2,3,1,0:T(8,128)S(1)} %copy.58, f32[1,16,64,256]{2,3,1,0:T(8,128)} %copy.57, f32[2,16,64,8]{2,3,1,0:T(8,128)S(1)} %collective-permute-done, f32[2,16,8,272]{2,3,1,0:T(8,128)} %copy.61), kind=kLoop, calls=%fused_computation.24 | loop fusion | flops 3481600 | bytes 5570560 | tf_op jit(solution)/shard_map/concatenate | solution.py:49
  128.6 2.6 copy-done.19
  135.7 4.8 collective-permute-start.5
  145.5 4.7 slice_bitcast_fusion
  150.2 9.6 %collective-permute-done.4 = f32[9,80,272]{2,1,0:T(8,128)} collective-permute-done((f32[9,80,272]{2,1,0:T(8,128)}, f32[9,80,272]{2,1,0:T(8,128)}, u32[]{:S(2)}, u32[]{:S(2)}) %collective-permute-start.4) | collective-permute-done | bytes 783392 | tf_op jit(solution)/shard_map/ppermute | solution.py:163
  182.3 7.9 %multiply_reduce_fusion.1 = (f32[6,2,64,256]{2,3,1,0:T(8,128)S(1)}, f32[6,2,64,256]{2,3,1,0:T(8,128)S(1)}) fusion(f32[6,2,8,64,256]{3,4,2,1,0:T(8,128)} %constant_dynamic-update-slice_fusion, f32[8]{0:T(128)S(1)} %copy-done.74, f32[8]{0:T(128)S(1)} %copy-done.75), kind=kLoop, calls=%fused_computation.1 | loop fusion | flops 5898240 | bytes 7864384 | tf_op jit(solution)/shard_map/reduce_sum | solution.py:115
  191.7 2.1 copy.120
  193.8 2.1 copy.118
  196.0 2.1 copy.119
  199.1 2.2 slice.858
  202.9 2.2 slice.856
  205.2 2.6 copy.121
  207.8 2.4 pad_maximum_fusion.3
  226.9 4.4 collective-permute-start.6
  234.6 5.3 collective-permute-done.7
  241.9 8.4 %collective-permute-start.9 = (f32[9,3,1,33]{3,2,1,0:T(1,128)S(1)}, f32[9,3,1,33]{3,2,1,0:T(1,128)S(1)}, u32[]{:S(2)}, u32[]{:S(2)}) collective-permute-start(f32[9,3,1,33]{3,2,1,0:T(1,128)S(1)} %get-tuple-element.126), channel_id=1, source_target_pairs={{16,0},{32,16},{48,32},{64,48},{80,64},{96,80},{112,96},{128,112},... | collective-permute-start | bytes 10700 | tf_op jit(solution)/shard_map/ppermute | solution.py:60
  252.0 4.6 collective-permute-start.10
  258.2 2.6 collective-permute-done.10
  260.8 4.7 collective-permute-done.11
  267.9 2.1 copy.78
  271.2 3.8 multiply_reduce_fusion.17
  275.2 2.9 multiply_reduce_fusion.16
  288.9 3.9 collective-permute-start.12
  294.4 4.4 collective-permute-done.13
  300.8 7.8 %collective-permute-done.14 = f32[3,3,1,33]{3,2,1,0:T(1,128)S(1)} collective-permute-done((f32[3,3,1,33]{3,2,1,0:T(1,128)S(1)}, f32[3,3,1,33]{3,2,1,0:T(1,128)S(1)}, u32[]{:S(2)}, u32[]{:S(2)}) %collective-permute-start.14) | collective-permute-done | bytes 1220 | tf_op jit(solution)/shard_map/ppermute | solution.py:59
  311.9 3.8 collective-permute-start.16
  317.6 4.3 collective-permute-done.17
  327.0 3.7 multiply_reduce_fusion.14
  330.8 2.1 multiply_reduce_fusion.13
  341.1 3.6 collective-permute-start.18
  346.3 4.2 collective-permute-done.19
  352.4 7.8 %collective-permute-done.20 = f32[3,3,1,33]{3,2,1,0:T(1,128)S(1)} collective-permute-done((f32[3,3,1,33]{3,2,1,0:T(1,128)S(1)}, f32[3,3,1,33]{3,2,1,0:T(1,128)S(1)}, u32[]{:S(2)}, u32[]{:S(2)}) %collective-permute-start.20) | collective-permute-done | bytes 1220 | tf_op jit(solution)/shard_map/ppermute | solution.py:59
  369.9 4.1 collective-permute-done.23
  378.9 3.8 multiply_reduce_fusion.11
  382.7 3.1 bitcast_subtract_fusion.1
  399.5 4.2 collective-permute-done.25
  405.7 7.8 %collective-permute-done.26 = f32[3,3,1,33]{3,2,1,0:T(1,128)S(1)} collective-permute-done((f32[3,3,1,33]{3,2,1,0:T(1,128)S(1)}, f32[3,3,1,33]{3,2,1,0:T(1,128)S(1)}, u32[]{:S(2)}, u32[]{:S(2)}) %collective-permute-start.26) | collective-permute-done | bytes 1220 | tf_op jit(solution)/shard_map/ppermute | solution.py:59
  416.9 2.2 collective-permute-start.28
  421.0 4.3 collective-permute-done.29
  429.8 3.7 multiply_reduce_fusion.8
  447.3 4.2 collective-permute-done.31
  453.5 7.8 %collective-permute-done.32 = f32[3,3,1,33]{3,2,1,0:T(1,128)S(1)} collective-permute-done((f32[3,3,1,33]{3,2,1,0:T(1,128)S(1)}, f32[3,3,1,33]{3,2,1,0:T(1,128)S(1)}, u32[]{:S(2)}, u32[]{:S(2)}) %collective-permute-start.32) | collective-permute-done | bytes 1220 | tf_op jit(solution)/shard_map/ppermute | solution.py:59
  468.6 4.3 collective-permute-done.35
  477.4 3.7 multiply_reduce_fusion.5
  481.1 2.1 multiply_reduce_fusion.4
  494.9 4.2 collective-permute-done.37
  501.1 7.8 %collective-permute-done.38 = f32[3,3,1,33]{3,2,1,0:T(1,128)S(1)} collective-permute-done((f32[3,3,1,33]{3,2,1,0:T(1,128)S(1)}, f32[3,3,1,33]{3,2,1,0:T(1,128)S(1)}, u32[]{:S(2)}, u32[]{:S(2)}) %collective-permute-start.38) | collective-permute-done | bytes 1220 | tf_op jit(solution)/shard_map/ppermute | solution.py:59
  516.2 4.3 collective-permute-done.41
  527.4 3.8 multiply_reduce_fusion.2
  531.2 2.9 bitcast_subtract_fusion
  (415 shorter events, 200.5 us)
Async XLA Ops:
  4.0 31.6 %all-to-all-start.1 = ((f32[1,1024,256]{2,0,1:T(1,128)}), f32[1,1024,256]{2,0,1:T(1,128)S(1)}, u32[]{:S(2)}, u32[]{:S(2)}) async-start(f32[1,1024,256]{2,0,1:T(1,128)} %copy.56), calls=%async_computation.1 | async-start | bytes 2097152 | tf_op jit(solution)/shard_map/all_to_all | solution.py:152
  35.6 24.8 %all-to-all-start = ((f32[1,1024,256]{2,0,1:T(1,128)}), f32[1,1024,256]{2,0,1:T(1,128)}, u32[]{:S(2)}, u32[]{:S(2)}) async-start(f32[1,1024,256]{2,0,1:T(1,128)} %copy.55), calls=%async_computation | async-start | bytes 2097152 | tf_op jit(solution)/shard_map/all_to_all | solution.py:151
  64.3 20.9 %copy-start.18 = (f32[1,16,64,256]{2,3,1,0:T(8,128)S(1)}, f32[1,16,64,256]{2,3,1,0:T(8,128)}, u32[]{:S(2)}) copy-start(f32[1,16,64,256]{2,3,1,0:T(8,128)} %copy.57) | copy-start | bytes 3145732
  65.4 18.7 %collective-permute-start.1 = (f32[2,16,64,8]{2,3,1,0:T(8,128)S(1)}, f32[2,16,64,8]{2,3,1,0:T(8,128)S(1)}, u32[]{:S(2)}, u32[]{:S(2)}) collective-permute-start(f32[2,16,64,8]{2,3,1,0:T(8,128)S(1)} %get-tuple-element.60), channel_id=1, source_target_pairs={{4,0},{8,4},{12,8},{5,1},{9,5},{13,9},{6,2},{10,6},{14,10},{7,3},{... | collective-permute-start | bytes 196616 | tf_op jit(solution)/shard_map/ppermute | solution.py:48
  66.7 18.6 %collective-permute-start = (f32[2,16,64,8]{2,3,1,0:T(8,128)S(1)}, f32[2,16,64,8]{2,3,1,0:T(8,128)S(1)}, u32[]{:S(2)}, u32[]{:S(2)}) collective-permute-start(f32[2,16,64,8]{2,3,1,0:T(8,128)S(1)} %get-tuple-element.59), channel_id=1, source_target_pairs={{0,4},{4,8},{8,12},{1,5},{5,9},{9,13},{2,6},{6,10},{10,14},{3,7},{... | collective-permute-start | bytes 196616 | tf_op jit(solution)/shard_map/ppermute | solution.py:47
  84.0 37.8 %copy-start.26 = (f32[2,16,64,8]{2,3,1,0:T(8,128)}, f32[2,16,64,8]{2,3,1,0:T(8,128)S(1)}, u32[]{:S(2)}) copy-start(f32[2,16,64,8]{2,3,1,0:T(8,128)S(1)} %collective-permute-done.1) | copy-start | bytes 196612
  85.2 36.6 %copy-start.28 = (f32[2,16,64,8]{2,3,1,0:T(8,128)}, f32[2,16,64,8]{2,3,1,0:T(8,128)S(1)}, u32[]{:S(2)}) copy-start(f32[2,16,64,8]{2,3,1,0:T(8,128)S(1)} %collective-permute-done) | copy-start | bytes 196612
  93.9 8.3 %collective-permute-start.3 = (f32[2,16,8,272]{3,2,1,0:T(8,128)S(1)}, f32[2,16,8,272]{3,2,1,0:T(8,128)S(1)}, u32[]{:S(2)}, u32[]{:S(2)}) collective-permute-start(f32[2,16,8,272]{3,2,1,0:T(8,128)S(1)} %copy.60), channel_id=1, source_target_pairs={{16,0},{32,16},{48,32},{64,48},{80,64},{96,80},{112,96},{128,112},... | collective-permute-start | bytes 835592 | tf_op jit(solution)/shard_map/ppermute | solution.py:48
  99.8 18.2 %collective-permute-start.2 = (f32[2,16,8,272]{3,2,1,0:T(8,128)}, f32[2,16,8,272]{3,2,1,0:T(8,128)}, u32[]{:S(2)}, u32[]{:S(2)}) collective-permute-start(f32[2,16,8,272]{3,2,1,0:T(8,128)} %copy.59), channel_id=1, source_target_pairs={{0,16},{16,32},{32,48},{48,64},{64,80},{80,96},{96,112},{112,128},... | collective-permute-start | bytes 835592 | tf_op jit(solution)/shard_map/ppermute | solution.py:47
  133.7 26.0 %collective-permute-start.4 = (f32[9,80,272]{2,1,0:T(8,128)}, f32[9,80,272]{2,1,0:T(8,128)}, u32[]{:S(2)}, u32[]{:S(2)}) collective-permute-start(f32[9,80,272]{2,1,0:T(8,128)} %copy.63), channel_id=1, source_target_pairs={{1,0},{2,1},{3,2},{5,4},{6,5},{7,6},{9,8},{10,9},{11,10},{13,12},{... | collective-permute-start | bytes 2350088 | tf_op jit(solution)/shard_map/ppermute | solution.py:163
  135.7 25.6 %collective-permute-start.5 = (f32[9,80,272]{2,1,0:T(8,128)S(1)}, f32[9,80,272]{2,1,0:T(8,128)S(1)}, u32[]{:S(2)}, u32[]{:S(2)}) collective-permute-start(f32[9,80,272]{2,1,0:T(8,128)S(1)} %copy.65), channel_id=1, source_target_pairs={{0,1},{1,2},{2,3},{4,5},{5,6},{6,7},{8,9},{9,10},{10,11},{12,13},{... | collective-permute-start | bytes 2350088 | tf_op jit(solution)/shard_map/ppermute | solution.py:162
  226.9 6.4 %collective-permute-start.6 = (f32[9,1,9,33]{3,2,1,0:T(8,128)S(1)}, f32[9,1,9,33]{3,2,1,0:T(8,128)S(1)}, u32[]{:S(2)}, u32[]{:S(2)}) collective-permute-start(f32[9,1,9,33]{3,2,1,0:T(8,128)S(1)} %fusion.60), channel_id=1, source_target_pairs={{0,1},{1,2},{2,3},{4,5},{5,6},{6,7},{8,9},{9,10},{10,11},{12,13},{... | collective-permute-start | bytes 32084 | tf_op jit(solution)/shard_map/ppermute | solution.py:59
  233.3 6.6 %collective-permute-start.7 = (f32[9,1,9,33]{3,2,1,0:T(8,128)S(1)}, f32[9,1,9,33]{3,2,1,0:T(8,128)S(1)}, u32[]{:S(2)}, u32[]{:S(2)}) collective-permute-start(f32[9,1,9,33]{3,2,1,0:T(8,128)S(1)} %get-tuple-element.42), channel_id=1, source_target_pairs={{1,0},{2,1},{3,2},{5,4},{6,5},{7,6},{9,8},{10,9},{11,10},{13,12},{... | collective-permute-start | bytes 32084 | tf_op jit(solution)/shard_map/ppermute | solution.py:60
  239.9 25.9 %copy-start.73 = (f32[6]{0:T(128)S(1)}, f32[6]{0:T(128)}, u32[]{:S(2)}) copy-start(f32[6]{0:T(128)} %constant.84) | copy-start | bytes 76
  240.0 10.4 %collective-permute-start.8 = (f32[9,3,1,33]{3,2,1,0:T(1,128)S(1)}, f32[9,3,1,33]{3,2,1,0:T(1,128)S(1)}, u32[]{:S(2)}, u32[]{:S(2)}) collective-permute-start(f32[9,3,1,33]{3,2,1,0:T(1,128)S(1)} %get-tuple-element.125), channel_id=1, source_target_pairs={{0,16},{16,32},{32,48},{48,64},{64,80},{80,96},{96,112},{112,128},... | collective-permute-start | bytes 10700 | tf_op jit(solution)/shard_map/ppermute | solution.py:59
  241.9 9.9 %collective-permute-start.9 = (f32[9,3,1,33]{3,2,1,0:T(1,128)S(1)}, f32[9,3,1,33]{3,2,1,0:T(1,128)S(1)}, u32[]{:S(2)}, u32[]{:S(2)}) collective-permute-start(f32[9,3,1,33]{3,2,1,0:T(1,128)S(1)} %get-tuple-element.126), channel_id=1, source_target_pairs={{16,0},{32,16},{48,32},{64,48},{80,64},{96,80},{112,96},{128,112},... | collective-permute-start | bytes 10700 | tf_op jit(solution)/shard_map/ppermute | solution.py:60
  252.0 8.8 %collective-permute-start.10 = (f32[9,3,9,1]{3,2,1,0:T(8,128)S(1)}, f32[9,3,9,1]{3,2,1,0:T(8,128)S(1)}, u32[]{:S(2)}, u32[]{:S(2)}) collective-permute-start(f32[9,3,9,1]{3,2,1,0:T(8,128)S(1)} %get-tuple-element.121), channel_id=1, source_target_pairs={{0,4},{4,8},{8,12},{1,5},{5,9},{9,13},{2,6},{6,10},{10,14},{3,7},{... | collective-permute-start | bytes 2924 | tf_op jit(solution)/shard_map/ppermute | solution.py:59
  256.6 8.8 %collective-permute-start.11 = (f32[9,3,9,1]{3,2,1,0:T(8,128)S(1)}, f32[9,3,9,1]{3,2,1,0:T(8,128)S(1)}, u32[]{:S(2)}, u32[]{:S(2)}) collective-permute-start(f32[9,3,9,1]{3,2,1,0:T(8,128)S(1)} %get-tuple-element.122), channel_id=1, source_target_pairs={{4,0},{8,4},{12,8},{5,1},{9,5},{13,9},{6,2},{10,6},{14,10},{7,3},{... | collective-permute-start | bytes 2924 | tf_op jit(solution)/shard_map/ppermute | solution.py:60
  288.9 5.4 %collective-permute-start.12 = (f32[3,1,9,33]{3,2,1,0:T(8,128)S(1)}, f32[3,1,9,33]{3,2,1,0:T(8,128)S(1)}, u32[]{:S(2)}, u32[]{:S(2)}) collective-permute-start(f32[3,1,9,33]{3,2,1,0:T(8,128)S(1)} %get-tuple-element.171), channel_id=1, source_target_pairs={{0,1},{1,2},{2,3},{4,5},{5,6},{6,7},{8,9},{9,10},{10,11},{12,13},{... | collective-permute-start | bytes 10700 | tf_op jit(solution)/shard_map/ppermute | solution.py:59
  292.8 5.9 %collective-permute-start.13 = (f32[3,1,9,33]{3,2,1,0:T(8,128)S(1)}, f32[3,1,9,33]{3,2,1,0:T(8,128)S(1)}, u32[]{:S(2)}, u32[]{:S(2)}) collective-permute-start(f32[3,1,9,33]{3,2,1,0:T(8,128)S(1)} %get-tuple-element.172), channel_id=1, source_target_pairs={{1,0},{2,1},{3,2},{5,4},{6,5},{7,6},{9,8},{10,9},{11,10},{13,12},{... | collective-permute-start | bytes 10700 | tf_op jit(solution)/shard_map/ppermute | solution.py:60
  298.8 9.7 %collective-permute-start.14 = (f32[3,3,1,33]{3,2,1,0:T(1,128)S(1)}, f32[3,3,1,33]{3,2,1,0:T(1,128)S(1)}, u32[]{:S(2)}, u32[]{:S(2)}) collective-permute-start(f32[3,3,1,33]{3,2,1,0:T(1,128)S(1)} %pad_maximum_fusion.30), channel_id=1, source_target_pairs={{0,16},{16,32},{32,48},{48,64},{64,80},{80,96},{96,112},{112,128},... | collective-permute-start | bytes 3572 | tf_op jit(solution)/shard_map/ppermute | solution.py:59
  308.5 3.2 collective-permute-start.15
  311.9 5.8 %collective-permute-start.16 = (f32[3,3,9,1]{3,2,1,0:T(8,128)S(1)}, f32[3,3,9,1]{3,2,1,0:T(8,128)S(1)}, u32[]{:S(2)}, u32[]{:S(2)}) collective-permute-start(f32[3,3,9,1]{3,2,1,0:T(8,128)S(1)} %get-tuple-element.166), channel_id=1, source_target_pairs={{0,4},{4,8},{8,12},{1,5},{5,9},{9,13},{2,6},{6,10},{10,14},{3,7},{... | collective-permute-start | bytes 980 | tf_op jit(solution)/shard_map/ppermute | solution.py:59
  315.7 6.2 %collective-permute-start.17 = (f32[3,3,9,1]{3,2,1,0:T(8,128)S(1)}, f32[3,3,9,1]{3,2,1,0:T(8,128)S(1)}, u32[]{:S(2)}, u32[]{:S(2)}) collective-permute-start(f32[3,3,9,1]{3,2,1,0:T(8,128)S(1)} %get-tuple-element.167), channel_id=1, source_target_pairs={{4,0},{8,4},{12,8},{5,1},{9,5},{13,9},{6,2},{10,6},{14,10},{7,3},{... | collective-permute-start | bytes 980 | tf_op jit(solution)/shard_map/ppermute | solution.py:60
  337.2 37.0 %copy-start.54 = (f32[1,3,9,33]{3,2,1,0:T(8,128)S(1)}, f32[1,3,9,33]{3,2,1,0:T(8,128)}, u32[]{:S(2)}) copy-start(f32[1,3,9,33]{3,2,1,0:T(8,128)} %copy-done.53) | copy-start | bytes 10696
  337.2 37.0 %copy-start.56 = (f32[1,3,9,33]{3,2,1,0:T(8,128)S(1)}, f32[1,3,9,33]{3,2,1,0:T(8,128)}, u32[]{:S(2)}) copy-start(f32[1,3,9,33]{3,2,1,0:T(8,128)} %copy-done.55) | copy-start | bytes 10696
  337.2 37.0 %copy-start.58 = (f32[1,3,9,33]{3,2,1,0:T(8,128)S(1)}, f32[1,3,9,33]{3,2,1,0:T(8,128)}, u32[]{:S(2)}) copy-start(f32[1,3,9,33]{3,2,1,0:T(8,128)} %copy-done.57) | copy-start | bytes 10696
  337.2 37.0 %copy-start.63 = (f32[3,3,9,33]{3,2,1,0:T(8,128)S(1)}, f32[3,3,9,33]{3,2,1,0:T(8,128)}, u32[]{:S(2)}) copy-start(f32[3,3,9,33]{3,2,1,0:T(8,128)} %get-tuple-element.31) | copy-start | bytes 32080
  341.1 5.1 collective-permute-start.18
  344.8 5.7 %collective-permute-start.19 = (f32[3,1,9,33]{3,2,1,0:T(8,128)S(1)}, f32[3,1,9,33]{3,2,1,0:T(8,128)S(1)}, u32[]{:S(2)}, u32[]{:S(2)}) collective-permute-start(f32[3,1,9,33]{3,2,1,0:T(8,128)S(1)} %get-tuple-element.163), channel_id=1, source_target_pairs={{1,0},{2,1},{3,2},{5,4},{6,5},{7,6},{9,8},{10,9},{11,10},{13,12},{... | collective-permute-start | bytes 10700 | tf_op jit(solution)/shard_map/ppermute | solution.py:60
  350.5 9.7 %collective-permute-start.20 = (f32[3,3,1,33]{3,2,1,0:T(1,128)S(1)}, f32[3,3,1,33]{3,2,1,0:T(1,128)S(1)}, u32[]{:S(2)}, u32[]{:S(2)}) collective-permute-start(f32[3,3,1,33]{3,2,1,0:T(1,128)S(1)} %pad_maximum_fusion.28), channel_id=1, source_target_pairs={{0,16},{16,32},{32,48},{48,64},{64,80},{80,96},{96,112},{112,128},... | collective-permute-start | bytes 3572 | tf_op jit(solution)/shard_map/ppermute | solution.py:59
  360.3 5.4 %collective-permute-start.21 = (f32[3,3,1,33]{3,2,1,0:T(1,128)S(1)}, f32[3,3,1,33]{3,2,1,0:T(1,128)S(1)}, u32[]{:S(2)}, u32[]{:S(2)}) collective-permute-start(f32[3,3,1,33]{3,2,1,0:T(1,128)S(1)} %get-tuple-element.29), channel_id=1, source_target_pairs={{16,0},{32,16},{48,32},{64,48},{80,64},{96,80},{112,96},{128,112},... | collective-permute-start | bytes 3572 | tf_op jit(solution)/shard_map/ppermute | solution.py:60
  365.8 4.1 collective-permute-start.22
  367.8 6.3 %collective-permute-start.23 = (f32[3,3,9,1]{3,2,1,0:T(8,128)S(1)}, f32[3,3,9,1]{3,2,1,0:T(8,128)S(1)}, u32[]{:S(2)}, u32[]{:S(2)}) collective-permute-start(f32[3,3,9,1]{3,2,1,0:T(8,128)S(1)} %get-tuple-element.158), channel_id=1, source_target_pairs={{4,0},{8,4},{12,8},{5,1},{9,5},{13,9},{6,2},{10,6},{14,10},{7,3},{... | collective-permute-start | bytes 980 | tf_op jit(solution)/shard_map/ppermute | solution.py:60
  396.1 3.4 collective-permute-start.24
  398.0 5.7 %collective-permute-start.25 = (f32[3,1,9,33]{3,2,1,0:T(8,128)S(1)}, f32[3,1,9,33]{3,2,1,0:T(8,128)S(1)}, u32[]{:S(2)}, u32[]{:S(2)}) collective-permute-start(f32[3,1,9,33]{3,2,1,0:T(8,128)S(1)} %get-tuple-element.154), channel_id=1, source_target_pairs={{1,0},{2,1},{3,2},{5,4},{6,5},{7,6},{9,8},{10,9},{11,10},{13,12},{... | collective-permute-start | bytes 10700 | tf_op jit(solution)/shard_map/ppermute | solution.py:60
  403.8 9.7 %collective-permute-start.26 = (f32[3,3,1,33]{3,2,1,0:T(1,128)S(1)}, f32[3,3,1,33]{3,2,1,0:T(1,128)S(1)}, u32[]{:S(2)}, u32[]{:S(2)}) collective-permute-start(f32[3,3,1,33]{3,2,1,0:T(1,128)S(1)} %pad_maximum_fusion.26), channel_id=1, source_target_pairs={{0,16},{16,32},{32,48},{48,64},{64,80},{80,96},{96,112},{112,128},... | collective-permute-start | bytes 3572 | tf_op jit(solution)/shard_map/ppermute | solution.py:59
  413.5 3.2 collective-permute-start.27
  416.9 4.2 collective-permute-start.28
  419.1 6.2 %collective-permute-start.29 = (f32[3,3,9,1]{3,2,1,0:T(8,128)S(1)}, f32[3,3,9,1]{3,2,1,0:T(8,128)S(1)}, u32[]{:S(2)}, u32[]{:S(2)}) collective-permute-start(f32[3,3,9,1]{3,2,1,0:T(8,128)S(1)} %get-tuple-element.149), channel_id=1, source_target_pairs={{4,0},{8,4},{12,8},{5,1},{9,5},{13,9},{6,2},{10,6},{14,10},{7,3},{... | collective-permute-start | bytes 980 | tf_op jit(solution)/shard_map/ppermute | solution.py:60
  439.9 33.0 %copy-start.31 = (f32[3,3,9,31]{3,2,1,0:T(8,128)S(1)}, f32[3,3,9,31]{3,2,1,0:T(8,128)}, u32[]{:S(2)}) copy-start(f32[3,3,9,31]{3,2,1,0:T(8,128)} %copy-done.30) | copy-start | bytes 30136
  439.9 33.0 %copy-start.34 = (f32[3,3,9,1]{3,2,1,0:T(8,128)S(1)}, f32[3,3,9,1]{3,2,1,0:T(8,128)}, u32[]{:S(2)}) copy-start(f32[3,3,9,1]{3,2,1,0:T(8,128)} %copy-done.33) | copy-start | bytes 976
  439.9 33.0 %copy-start.37 = (f32[3,3,9,1]{3,2,1,0:T(8,128)S(1)}, f32[3,3,9,1]{3,2,1,0:T(8,128)}, u32[]{:S(2)}) copy-start(f32[3,3,9,1]{3,2,1,0:T(8,128)} %copy-done.36) | copy-start | bytes 976
  439.9 33.0 %copy-start.42 = (f32[1,3,9,33]{3,2,1,0:T(8,128)S(1)}, f32[1,3,9,33]{3,2,1,0:T(8,128)}, u32[]{:S(2)}) copy-start(f32[1,3,9,33]{3,2,1,0:T(8,128)} %copy-done.41) | copy-start | bytes 10696
  439.9 33.0 %copy-start.45 = (f32[1,3,9,33]{3,2,1,0:T(8,128)S(1)}, f32[1,3,9,33]{3,2,1,0:T(8,128)}, u32[]{:S(2)}) copy-start(f32[1,3,9,33]{3,2,1,0:T(8,128)} %copy-done.44) | copy-start | bytes 10696
  440.0 33.0 %copy-start.48 = (f32[1,3,9,33]{3,2,1,0:T(8,128)S(1)}, f32[1,3,9,33]{3,2,1,0:T(8,128)}, u32[]{:S(2)}) copy-start(f32[1,3,9,33]{3,2,1,0:T(8,128)} %copy-done.47) | copy-start | bytes 10696
  443.9 3.4 collective-permute-start.30
  445.8 5.7 %collective-permute-start.31 = (f32[3,1,9,33]{3,2,1,0:T(8,128)S(1)}, f32[3,1,9,33]{3,2,1,0:T(8,128)S(1)}, u32[]{:S(2)}, u32[]{:S(2)}) collective-permute-start(f32[3,1,9,33]{3,2,1,0:T(8,128)S(1)} %get-tuple-element.145), channel_id=1, source_target_pairs={{1,0},{2,1},{3,2},{5,4},{6,5},{7,6},{9,8},{10,9},{11,10},{13,12},{... | collective-permute-start | bytes 10700 | tf_op jit(solution)/shard_map/ppermute | solution.py:60
  451.6 9.7 %collective-permute-start.32 = (f32[3,3,1,33]{3,2,1,0:T(1,128)S(1)}, f32[3,3,1,33]{3,2,1,0:T(1,128)S(1)}, u32[]{:S(2)}, u32[]{:S(2)}) collective-permute-start(f32[3,3,1,33]{3,2,1,0:T(1,128)S(1)} %pad_maximum_fusion.24), channel_id=1, source_target_pairs={{0,16},{16,32},{32,48},{48,64},{64,80},{80,96},{96,112},{112,128},... | collective-permute-start | bytes 3572 | tf_op jit(solution)/shard_map/ppermute | solution.py:59
  461.3 3.2 collective-permute-start.33
  464.7 3.9 collective-permute-start.34
  466.6 6.2 %collective-permute-start.35 = (f32[3,3,9,1]{3,2,1,0:T(8,128)S(1)}, f32[3,3,9,1]{3,2,1,0:T(8,128)S(1)}, u32[]{:S(2)}, u32[]{:S(2)}) collective-permute-start(f32[3,3,9,1]{3,2,1,0:T(8,128)S(1)} %get-tuple-element.140), channel_id=1, source_target_pairs={{4,0},{8,4},{12,8},{5,1},{9,5},{13,9},{6,2},{10,6},{14,10},{7,3},{... | collective-permute-start | bytes 980 | tf_op jit(solution)/shard_map/ppermute | solution.py:60
  487.5 33.0 %copy-start.32 = (f32[3,3,9,31]{3,2,1,0:T(8,128)S(1)}, f32[3,3,9,31]{3,2,1,0:T(8,128)}, u32[]{:S(2)}) copy-start(f32[3,3,9,31]{3,2,1,0:T(8,128)} %copy-done.30) | copy-start | bytes 30136
  487.5 33.0 %copy-start.35 = (f32[3,3,9,1]{3,2,1,0:T(8,128)S(1)}, f32[3,3,9,1]{3,2,1,0:T(8,128)}, u32[]{:S(2)}) copy-start(f32[3,3,9,1]{3,2,1,0:T(8,128)} %copy-done.33) | copy-start | bytes 976
  487.5 33.0 %copy-start.38 = (f32[3,3,9,1]{3,2,1,0:T(8,128)S(1)}, f32[3,3,9,1]{3,2,1,0:T(8,128)}, u32[]{:S(2)}) copy-start(f32[3,3,9,1]{3,2,1,0:T(8,128)} %copy-done.36) | copy-start | bytes 976
  487.5 33.1 %copy-start.43 = (f32[1,3,9,33]{3,2,1,0:T(8,128)S(1)}, f32[1,3,9,33]{3,2,1,0:T(8,128)}, u32[]{:S(2)}) copy-start(f32[1,3,9,33]{3,2,1,0:T(8,128)} %copy-done.41) | copy-start | bytes 10696
  487.5 33.1 %copy-start.46 = (f32[1,3,9,33]{3,2,1,0:T(8,128)S(1)}, f32[1,3,9,33]{3,2,1,0:T(8,128)}, u32[]{:S(2)}) copy-start(f32[1,3,9,33]{3,2,1,0:T(8,128)} %copy-done.44) | copy-start | bytes 10696
  487.5 33.1 %copy-start.49 = (f32[1,3,9,33]{3,2,1,0:T(8,128)S(1)}, f32[1,3,9,33]{3,2,1,0:T(8,128)}, u32[]{:S(2)}) copy-start(f32[1,3,9,33]{3,2,1,0:T(8,128)} %copy-done.47) | copy-start | bytes 10696
  491.5 3.4 collective-permute-start.36
  493.4 5.7 %collective-permute-start.37 = (f32[3,1,9,33]{3,2,1,0:T(8,128)S(1)}, f32[3,1,9,33]{3,2,1,0:T(8,128)S(1)}, u32[]{:S(2)}, u32[]{:S(2)}) collective-permute-start(f32[3,1,9,33]{3,2,1,0:T(8,128)S(1)} %get-tuple-element.136), channel_id=1, source_target_pairs={{1,0},{2,1},{3,2},{5,4},{6,5},{7,6},{9,8},{10,9},{11,10},{13,12},{... | collective-permute-start | bytes 10700 | tf_op jit(solution)/shard_map/ppermute | solution.py:60
  499.2 9.7 %collective-permute-start.38 = (f32[3,3,1,33]{3,2,1,0:T(1,128)S(1)}, f32[3,3,1,33]{3,2,1,0:T(1,128)S(1)}, u32[]{:S(2)}, u32[]{:S(2)}) collective-permute-start(f32[3,3,1,33]{3,2,1,0:T(1,128)S(1)} %pad_maximum_fusion.22), channel_id=1, source_target_pairs={{0,16},{16,32},{32,48},{48,64},{64,80},{80,96},{96,112},{112,128},... | collective-permute-start | bytes 3572 | tf_op jit(solution)/shard_map/ppermute | solution.py:59
  508.9 3.2 collective-permute-start.39
  512.3 3.9 collective-permute-start.40
  514.2 6.2 %collective-permute-start.41 = (f32[3,3,9,1]{3,2,1,0:T(8,128)S(1)}, f32[3,3,9,1]{3,2,1,0:T(8,128)S(1)}, u32[]{:S(2)}, u32[]{:S(2)}) collective-permute-start(f32[3,3,9,1]{3,2,1,0:T(8,128)S(1)} %get-tuple-element.131), channel_id=1, source_target_pairs={{4,0},{8,4},{12,8},{5,1},{9,5},{13,9},{6,2},{10,6},{14,10},{7,3},{... | collective-permute-start | bytes 980 | tf_op jit(solution)/shard_map/ppermute | solution.py:60
  (58 other events, 195.0 us)
where the time goes:
time: 546 us; the launch traced here: 536 us
  waiting for transfers between devices  167 us (31%)
  local copies, waits for them, and re-layouts  131 us (24%)
  starting transfers between devices  125 us (23%)
  other arithmetic  84.1 us (15%)
  matrix products  17.5 us (3%)
  between operations  10.5 us (2%)
    unnamed x199, local copies, waits for them, and re-layouts  60.4 us
    ppermute x18, waiting for transfers between devices, share(): from_high = lax.ppermute(first, axis, backward)  59.1 us
    ppermute x18, waiting for transfers between devices, share(): from_low = lax.ppermute(last, axis, forward)  47.2 us
    ppermute x18, starting transfers between devices, share(): from_low = lax.ppermute(last, axis, forward)  45.6 us
    ppermute x18, starting transfers between devices, share(): from_high = lax.ppermute(first, axis, backward)  34.2 us
    reduce_sum x7, other arithmetic, reduce_z(): low = jnp.sum(blocks * lower.reshape(shape), axis=2)  21.4 us
    all_to_all x1, waiting for transfers between devices, bricks_of(): lax.all_to_all(deformed_slab, 'gx', split_axis=1, concat_axis=0, tiled=True)  18 us
    ppermute x2, starting transfers between devices, halo(): lax.ppermute(lax.slice_in_dim(block, size - width, size, axis=dim), axis,...  18 us
  transfers between devices with their start and end apart: 44, of which 41 were waited for; matrix products, arithmetic and copies ran while one was open for 3% of the time, Pallas kernels for 0%

commit v1 on v0

--- a/solution.py
+++ b/solution.py
@@ -148,7 +148,10 @@
 
 
 def bricks_of(image_slab, deformed_slab):
-    image = lax.all_to_all(image_slab, "gx", split_axis=1, concat_axis=0, tiled=True)
+    image = jnp.concatenate(
+        lax.all_to_all(jnp.stack(jnp.split(image_slab, lax.axis_size("gx"), axis=1)), "gx", 0, 0),
+        axis=0,
+    )
     deformed = lax.all_to_all(deformed_slab, "gx", split_axis=1, concat_axis=0, tiled=True)
     both = jnp.stack([image, deformed])
     both = halo(both, "gy", 3, DMAX)

time: 546 us -> 387 us (0.71)
  local copies, waits for them, and re-layouts: 131 us -> 31.7 us
  other arithmetic: 84.1 us -> 31 us
  matrix products: 17.5 us -> 11.5 us
    unnamed x199 -> x75, local copies, waits for them, and re-layouts: 60.4 us -> 19.2 us
    slice x18 -> x0, local copies, waits for them, and re-layouts: 19.9 us -> none  [the longest x6 8.43 us: expand_z(): high = values[:, 1:, None]]
    reduce_sum x7, other arithmetic: 21.4 us -> 4.69 us  [reduce_z(): low = jnp.sum(blocks * lower.reshape(shape), axis=2)]
    reduce_sum x4, other arithmetic: 15 us -> 2.53 us  [operator(): inner = jnp.sum(grads * interpolate(delta, tables, weights), axis=0)]
    slice x12 -> x6, local copies, waits for them, and re-layouts: 11.8 us -> 0.44 us  [expand_z(): low = values[:, :count, None]]
    all_to_all x1, waiting for transfers between devices: 18 us -> 9.97 us  [bricks_of(): lax.all_to_all(deformed_slab, 'gx', split_axis=1, concat_axis=0, tiled=True)]
    slice x2 -> x1, local copies, waits for them, and re-layouts: 8.98 us -> 1.53 us  [halo(): lax.slice_in_dim(block, size - width, size, axis=dim)]
    dot_general x7, matrix products: 9.98 us -> 3.26 us  [restrict(): step = jnp.einsum('caxy,xb->caby', step, table_x, precision=HI)]
  transfers between devices with their start and end apart: 44 -> 44, of which waited for: 41 -> 41; matrix products, arithmetic and copies ran while one was open for 3% -> 4% of each run, Pallas kernels for 0% -> 0%
where the time goes in v1:
time: 387 us; the launch traced here: 381 us
  waiting for transfers between devices  169 us (44%)
  starting transfers between devices  128 us (33%)
  local copies, waits for them, and re-layouts  31.7 us (8%)
  other arithmetic  31 us (8%)
  matrix products  11.5 us (3%)
  between operations  10 us (3%)
    ppermute x18, waiting for transfers between devices, share(): from_high = lax.ppermute(first, axis, backward)  59.1 us
    ppermute x18, waiting for transfers between devices, share(): from_low = lax.ppermute(last, axis, forward)  47.9 us
    ppermute x18, starting transfers between devices, share(): from_low = lax.ppermute(last, axis, forward)  43.1 us
    ppermute x18, starting transfers between devices, share(): from_high = lax.ppermute(first, axis, backward)  33.9 us
    unnamed x75, local copies, waits for them, and re-layouts  19.2 us
    all_to_all x1, waiting for transfers between devices, bricks_of(): lax.all_to_all(jnp.stack(jnp.split(image_slab, lax.axis_size('gx'), axis=...  17.8 us
    ppermute x2, starting transfers between devices, halo(): lax.ppermute(lax.slice_in_dim(block, size - width, size, axis=dim), axis,...  16.9 us
    ppermute x2, waiting for transfers between devices, halo(): lax.ppermute(lax.slice_in_dim(block, size - width, size, axis=dim), axis,...  13.2 us
  transfers between devices with their start and end apart: 44, of which 41 were waited for; matrix products, arithmetic and copies ran while one was open for 4% of the time, Pallas kernels for 0%

profile of v1, /device:TPU:4, one launch (start us, length us, event | category | flops | bytes accessed | tf_op | source)
XLA Modules:
  0.0 381.2 jit_solution(16500483398206271821)
XLA Ops:
  0.6 3.4 copy.43
  4.0 11.4 %all-to-all-start.1 = ((f32[1,1024,256]{2,0,1:T(1,128)}), f32[1,1024,256]{2,0,1:T(1,128)S(1)}, u32[]{:S(2)}, u32[]{:S(2)}) async-start(f32[1,1024,256]{2,0,1:T(1,128)} %copy.43), calls=%async_computation.1 | async-start | bytes 2097152 | tf_op jit(solution)/shard_map/all_to_all | solution.py:155
  25.6 10.0 %all-to-all-done.1 = f32[1,1024,256]{2,0,1:T(1,128)S(1)} async-done(((f32[1,1024,256]{2,0,1:T(1,128)}), f32[1,1024,256]{2,0,1:T(1,128)S(1)}, u32[]{:S(2)}, u32[]{:S(2)}) %all-to-all-start.1) | async-done | bytes 1048608 | tf_op jit(solution)/shard_map/all_to_all | solution.py:155
  35.6 6.2 %all-to-all-start = ((f32[16,1,64,256]{3,2,1,0:T(8,128)}), f32[16,1,64,256]{3,2,1,0:T(8,128)S(1)}, u32[]{:S(2)}, u32[]{:S(2)}) async-start(f32[16,1,64,256]{3,2,1,0:T(8,128)} %bitcast_dynamic-update-slice_fusion), calls=%async_computation | async-start | bytes 2097152 | tf_op jit(solution)/shard_map/all_to_all | solution.py:152
  41.8 17.8 %all-to-all-done = f32[16,1,64,256]{3,2,1,0:T(8,128)S(1)} async-done(((f32[16,1,64,256]{3,2,1,0:T(8,128)}), f32[16,1,64,256]{3,2,1,0:T(8,128)S(1)}, u32[]{:S(2)}, u32[]{:S(2)}) %all-to-all-start) | async-done | bytes 1048608 | tf_op jit(solution)/shard_map/all_to_all | solution.py:152
  61.0 1.5 copy.44
  62.6 15.0 %collective-permute-start = (f32[2,16,64,8]{2,3,1,0:T(8,128)S(1)}, f32[2,16,64,8]{2,3,1,0:T(8,128)S(1)}, u32[]{:S(2)}, u32[]{:S(2)}) collective-permute-start(f32[2,16,64,8]{2,3,1,0:T(8,128)S(1)} %copy.44), channel_id=1, source_target_pairs={{0,4},{4,8},{8,12},{1,5},{5,9},{9,13},{2,6},{6,10},{10,14},{3,7},{... | collective-permute-start | bytes 196616 | tf_op jit(solution)/shard_map/ppermute | solution.py:47
  80.9 5.1 %collective-permute-done.1 = f32[2,16,64,8]{2,3,1,0:T(8,128)} collective-permute-done((f32[2,16,64,8]{2,3,1,0:T(8,128)}, f32[2,16,64,8]{2,3,1,0:T(8,128)}, u32[]{:S(2)}, u32[]{:S(2)}) %collective-permute-start.1) | collective-permute-done | bytes 65568 | tf_op jit(solution)/shard_map/ppermute | solution.py:48
  85.9 2.2 copy.47
  89.5 1.9 collective-permute-start.2
  91.5 8.4 %collective-permute-start.3 = (f32[2,16,8,272]{3,2,1,0:T(8,128)S(1)}, f32[2,16,8,272]{3,2,1,0:T(8,128)S(1)}, u32[]{:S(2)}, u32[]{:S(2)}) collective-permute-start(f32[2,16,8,272]{3,2,1,0:T(8,128)S(1)} %get-tuple-element.51), channel_id=1, source_target_pairs={{16,0},{32,16},{48,32},{64,48},{80,64},{96,80},{112,96},{128,112},... | collective-permute-start | bytes 835592 | tf_op jit(solution)/shard_map/ppermute | solution.py:48
  99.9 12.5 %collective-permute-done.2 = f32[2,16,8,272]{3,2,1,0:T(8,128)S(1)} collective-permute-done((f32[2,16,8,272]{3,2,1,0:T(8,128)S(1)}, f32[2,16,8,272]{3,2,1,0:T(8,128)S(1)}, u32[]{:S(2)}, u32[]{:S(2)}) %collective-permute-start.2) | collective-permute-done | bytes 278560 | tf_op jit(solution)/shard_map/ppermute | solution.py:47
  112.5 1.8 pad_maximum_fusion
  114.6 1.6 copy-done.2
  118.7 5.1 %collective-permute-start.5 = (f32[9,80,272]{2,1,0:T(8,128)}, f32[9,80,272]{2,1,0:T(8,128)S(1)}, u32[]{:S(2)}, u32[]{:S(2)}) collective-permute-start(f32[9,80,272]{2,1,0:T(8,128)} %pad_maximum_fusion.7), channel_id=1, source_target_pairs={{0,1},{1,2},{2,3},{4,5},{5,6},{6,7},{8,9},{9,10},{10,11},{12,13},{... | collective-permute-start | bytes 2350088 | tf_op jit(solution)/shard_map/ppermute | solution.py:165
  129.0 2.4 slice_bitcast_fusion
  131.4 13.0 %collective-permute-done.4 = f32[9,80,272]{2,1,0:T(8,128)S(1)} collective-permute-done((f32[9,80,272]{2,1,0:T(8,128)S(1)}, f32[9,80,272]{2,1,0:T(8,128)S(1)}, u32[]{:S(2)}, u32[]{:S(2)}) %collective-permute-start.4) | collective-permute-done | bytes 783392 | tf_op jit(solution)/shard_map/ppermute | solution.py:166
  144.4 3.1 collective-permute-done.5
  162.2 4.3 %collective-permute-start.6 = (f32[9,1,9,33]{3,2,1,0:T(8,128)S(1)}, f32[9,1,9,33]{3,2,1,0:T(8,128)S(1)}, u32[]{:S(2)}, u32[]{:S(2)}) collective-permute-start(f32[9,1,9,33]{3,2,1,0:T(8,128)S(1)} %fusion.61), channel_id=1, source_target_pairs={{0,1},{1,2},{2,3},{4,5},{5,6},{6,7},{8,9},{9,10},{10,11},{12,13},{... | collective-permute-start | bytes 32084 | tf_op jit(solution)/shard_map/ppermute | solution.py:59
  166.5 2.3 collective-permute-done.6
  170.2 5.4 %collective-permute-done.7 = f32[9,1,9,33]{3,2,1,0:T(8,128)S(1)} collective-permute-done((f32[9,1,9,33]{3,2,1,0:T(8,128)S(1)}, f32[9,1,9,33]{3,2,1,0:T(8,128)S(1)}, u32[]{:S(2)}, u32[]{:S(2)}) %collective-permute-start.7) | collective-permute-done | bytes 10724 | tf_op jit(solution)/shard_map/ppermute | solution.py:60
  175.6 1.9 collective-permute-start.8
  177.6 8.4 %collective-permute-start.9 = (f32[9,3,1,33]{3,2,1,0:T(1,128)S(1)}, f32[9,3,1,33]{3,2,1,0:T(1,128)S(1)}, u32[]{:S(2)}, u32[]{:S(2)}) collective-permute-start(f32[9,3,1,33]{3,2,1,0:T(1,128)S(1)} %get-tuple-element.119), channel_id=1, source_target_pairs={{16,0},{32,16},{48,32},{64,48},{80,64},{96,80},{112,96},{128,112},... | collective-permute-start | bytes 10700 | tf_op jit(solution)/shard_map/ppermute | solution.py:60
  187.6 2.9 collective-permute-start.10
  192.1 3.0 collective-permute-done.10
  195.1 4.1 %collective-permute-done.11 = f32[9,3,9,1]{3,2,1,0:T(8,128)S(1)} collective-permute-done((f32[9,3,9,1]{3,2,1,0:T(8,128)S(1)}, f32[9,3,9,1]{3,2,1,0:T(8,128)S(1)}, u32[]{:S(2)}, u32[]{:S(2)}) %collective-permute-start.11) | collective-permute-done | bytes 1004 | tf_op jit(solution)/shard_map/ppermute | solution.py:60
  203.0 3.9 %collective-permute-start.12 = (f32[3,1,9,33]{3,2,1,0:T(8,128)S(1)}, f32[3,1,9,33]{3,2,1,0:T(8,128)S(1)}, u32[]{:S(2)}, u32[]{:S(2)}) collective-permute-start(f32[3,1,9,33]{3,2,1,0:T(8,128)S(1)} %get-tuple-element.164), channel_id=1, source_target_pairs={{0,1},{1,2},{2,3},{4,5},{5,6},{6,7},{8,9},{9,10},{10,11},{12,13},{... | collective-permute-start | bytes 10700 | tf_op jit(solution)/shard_map/ppermute | solution.py:59
  208.4 4.2 %collective-permute-done.13 = f32[3,1,9,33]{3,2,1,0:T(8,128)S(1)} collective-permute-done((f32[3,1,9,33]{3,2,1,0:T(8,128)S(1)}, f32[3,1,9,33]{3,2,1,0:T(8,128)S(1)}, u32[]{:S(2)}, u32[]{:S(2)}) %collective-permute-start.13) | collective-permute-done | bytes 3596 | tf_op jit(solution)/shard_map/ppermute | solution.py:60
  212.6 1.9 collective-permute-start.14
  214.6 7.8 %collective-permute-done.14 = f32[3,3,1,33]{3,2,1,0:T(1,128)S(1)} collective-permute-done((f32[3,3,1,33]{3,2,1,0:T(1,128)S(1)}, f32[3,3,1,33]{3,2,1,0:T(1,128)S(1)}, u32[]{:S(2)}, u32[]{:S(2)}) %collective-permute-start.14) | collective-permute-done | bytes 1220 | tf_op jit(solution)/shard_map/ppermute | solution.py:59
  222.4 1.9 collective-permute-start.15
  225.7 3.0 collective-permute-start.16
  230.8 4.3 %collective-permute-done.17 = f32[3,3,9,1]{3,2,1,0:T(8,128)S(1)} collective-permute-done((f32[3,3,9,1]{3,2,1,0:T(8,128)S(1)}, f32[3,3,9,1]{3,2,1,0:T(8,128)S(1)}, u32[]{:S(2)}, u32[]{:S(2)}) %collective-permute-start.17) | collective-permute-done | bytes 356 | tf_op jit(solution)/shard_map/ppermute | solution.py:60
  239.3 3.5 collective-permute-start.18
  244.3 4.2 %collective-permute-done.19 = f32[3,1,9,33]{3,2,1,0:T(8,128)S(1)} collective-permute-done((f32[3,1,9,33]{3,2,1,0:T(8,128)S(1)}, f32[3,1,9,33]{3,2,1,0:T(8,128)S(1)}, u32[]{:S(2)}, u32[]{:S(2)}) %collective-permute-start.19) | collective-permute-done | bytes 3596 | tf_op jit(solution)/shard_map/ppermute | solution.py:60
  248.6 1.9 collective-permute-start.20
  250.5 7.8 %collective-permute-done.20 = f32[3,3,1,33]{3,2,1,0:T(1,128)S(1)} collective-permute-done((f32[3,3,1,33]{3,2,1,0:T(1,128)S(1)}, f32[3,3,1,33]{3,2,1,0:T(1,128)S(1)}, u32[]{:S(2)}, u32[]{:S(2)}) %collective-permute-start.20) | collective-permute-done | bytes 1220 | tf_op jit(solution)/shard_map/ppermute | solution.py:59
  258.4 1.9 collective-permute-start.21
  265.5 2.8 collective-permute-start.22
  270.1 4.7 %collective-permute-done.23 = f32[3,3,9,1]{3,2,1,0:T(8,128)} collective-permute-done((f32[3,3,9,1]{3,2,1,0:T(8,128)}, f32[3,3,9,1]{3,2,1,0:T(8,128)}, u32[]{:S(2)}, u32[]{:S(2)}) %collective-permute-start.23) | collective-permute-done | bytes 356 | tf_op jit(solution)/shard_map/ppermute | solution.py:60
  278.7 1.7 multiply_reduce_fusion.11
  283.3 2.0 collective-permute-start.24
  286.8 4.2 %collective-permute-done.25 = f32[3,1,9,33]{3,2,1,0:T(8,128)S(1)} collective-permute-done((f32[3,1,9,33]{3,2,1,0:T(8,128)S(1)}, f32[3,1,9,33]{3,2,1,0:T(8,128)S(1)}, u32[]{:S(2)}, u32[]{:S(2)}) %collective-permute-start.25) | collective-permute-done | bytes 3596 | tf_op jit(solution)/shard_map/ppermute | solution.py:60
  291.1 1.9 collective-permute-start.26
  293.0 7.8 %collective-permute-done.26 = f32[3,3,1,33]{3,2,1,0:T(1,128)S(1)} collective-permute-done((f32[3,3,1,33]{3,2,1,0:T(1,128)S(1)}, f32[3,3,1,33]{3,2,1,0:T(1,128)S(1)}, u32[]{:S(2)}, u32[]{:S(2)}) %collective-permute-start.26) | collective-permute-done | bytes 1220 | tf_op jit(solution)/shard_map/ppermute | solution.py:59
  300.8 1.9 collective-permute-start.27
  304.2 1.6 collective-permute-start.28
  305.7 1.5 collective-permute-start.29
  307.7 4.3 %collective-permute-done.29 = f32[3,3,9,1]{3,2,1,0:T(8,128)S(1)} collective-permute-done((f32[3,3,9,1]{3,2,1,0:T(8,128)S(1)}, f32[3,3,9,1]{3,2,1,0:T(8,128)S(1)}, u32[]{:S(2)}, u32[]{:S(2)}) %collective-permute-start.29) | collective-permute-done | bytes 356 | tf_op jit(solution)/shard_map/ppermute | solution.py:60
  315.3 1.9 collective-permute-start.30
  318.7 4.2 %collective-permute-done.31 = f32[3,1,9,33]{3,2,1,0:T(8,128)S(1)} collective-permute-done((f32[3,1,9,33]{3,2,1,0:T(8,128)S(1)}, f32[3,1,9,33]{3,2,1,0:T(8,128)S(1)}, u32[]{:S(2)}, u32[]{:S(2)}) %collective-permute-start.31) | collective-permute-done | bytes 3596 | tf_op jit(solution)/shard_map/ppermute | solution.py:60
  323.0 1.9 collective-permute-start.32
  324.9 7.8 %collective-permute-done.32 = f32[3,3,1,33]{3,2,1,0:T(1,128)S(1)} collective-permute-done((f32[3,3,1,33]{3,2,1,0:T(1,128)S(1)}, f32[3,3,1,33]{3,2,1,0:T(1,128)S(1)}, u32[]{:S(2)}, u32[]{:S(2)}) %collective-permute-start.32) | collective-permute-done | bytes 1220 | tf_op jit(solution)/shard_map/ppermute | solution.py:59
  332.7 1.9 collective-permute-start.33
  336.1 1.9 collective-permute-start.34
  340.0 4.3 %collective-permute-done.35 = f32[3,3,9,1]{3,2,1,0:T(8,128)S(1)} collective-permute-done((f32[3,3,9,1]{3,2,1,0:T(8,128)S(1)}, f32[3,3,9,1]{3,2,1,0:T(8,128)S(1)}, u32[]{:S(2)}, u32[]{:S(2)}) %collective-permute-start.35) | collective-permute-done | bytes 356 | tf_op jit(solution)/shard_map/ppermute | solution.py:60
  347.6 1.9 collective-permute-start.36
  351.0 4.2 %collective-permute-done.37 = f32[3,1,9,33]{3,2,1,0:T(8,128)S(1)} collective-permute-done((f32[3,1,9,33]{3,2,1,0:T(8,128)S(1)}, f32[3,1,9,33]{3,2,1,0:T(8,128)S(1)}, u32[]{:S(2)}, u32[]{:S(2)}) %collective-permute-start.37) | collective-permute-done | bytes 3596 | tf_op jit(solution)/shard_map/ppermute | solution.py:60
  355.3 1.9 collective-permute-start.38
  357.2 7.8 %collective-permute-done.38 = f32[3,3,1,33]{3,2,1,0:T(1,128)S(1)} collective-permute-done((f32[3,3,1,33]{3,2,1,0:T(1,128)S(1)}, f32[3,3,1,33]{3,2,1,0:T(1,128)S(1)}, u32[]{:S(2)}, u32[]{:S(2)}) %collective-permute-start.38) | collective-permute-done | bytes 1220 | tf_op jit(solution)/shard_map/ppermute | solution.py:59
  365.0 1.9 collective-permute-start.39
  368.4 1.9 collective-permute-start.40
  372.3 4.3 %collective-permute-done.41 = f32[3,3,9,1]{3,2,1,0:T(8,128)S(1)} collective-permute-done((f32[3,3,9,1]{3,2,1,0:T(8,128)S(1)}, f32[3,3,9,1]{3,2,1,0:T(8,128)S(1)}, u32[]{:S(2)}, u32[]{:S(2)}) %collective-permute-start.41) | collective-permute-done | bytes 356 | tf_op jit(solution)/shard_map/ppermute | solution.py:60
  379.3 1.6 bitcast_subtract_fusion
  (264 shorter events, 85.7 us)
Async XLA Ops:
  0.6 14.9 %copy-start.10 = (f32[1,1024,256]{2,1,0:T(8,128)S(1)}, f32[1,1024,256]{2,1,0:T(8,128)}, u32[]{:S(2)}) copy-start(f32[1,1024,256]{2,1,0:T(8,128)} %param.34) | copy-start | bytes 3145732
  4.0 31.6 %all-to-all-start.1 = ((f32[1,1024,256]{2,0,1:T(1,128)}), f32[1,1024,256]{2,0,1:T(1,128)S(1)}, u32[]{:S(2)}, u32[]{:S(2)}) async-start(f32[1,1024,256]{2,0,1:T(1,128)} %copy.43), calls=%async_computation.1 | async-start | bytes 2097152 | tf_op jit(solution)/shard_map/all_to_all | solution.py:155
  35.6 24.1 %all-to-all-start = ((f32[16,1,64,256]{3,2,1,0:T(8,128)}), f32[16,1,64,256]{3,2,1,0:T(8,128)S(1)}, u32[]{:S(2)}, u32[]{:S(2)}) async-start(f32[16,1,64,256]{3,2,1,0:T(8,128)} %bitcast_dynamic-update-slice_fusion), calls=%async_computation | async-start | bytes 2097152 | tf_op jit(solution)/shard_map/all_to_all | solution.py:152
  62.6 17.9 %collective-permute-start = (f32[2,16,64,8]{2,3,1,0:T(8,128)S(1)}, f32[2,16,64,8]{2,3,1,0:T(8,128)S(1)}, u32[]{:S(2)}, u32[]{:S(2)}) collective-permute-start(f32[2,16,64,8]{2,3,1,0:T(8,128)S(1)} %copy.44), channel_id=1, source_target_pairs={{0,4},{4,8},{8,12},{1,5},{5,9},{9,13},{2,6},{6,10},{10,14},{3,7},{... | collective-permute-start | bytes 196616 | tf_op jit(solution)/shard_map/ppermute | solution.py:47
  78.6 7.3 %collective-permute-start.1 = (f32[2,16,64,8]{2,3,1,0:T(8,128)}, f32[2,16,64,8]{2,3,1,0:T(8,128)}, u32[]{:S(2)}, u32[]{:S(2)}) collective-permute-start(f32[2,16,64,8]{2,3,1,0:T(8,128)} %copy.45), channel_id=1, source_target_pairs={{4,0},{8,4},{12,8},{5,1},{9,5},{13,9},{6,2},{10,6},{14,10},{7,3},{... | collective-permute-start | bytes 196616 | tf_op jit(solution)/shard_map/ppermute | solution.py:48
  88.1 24.3 %copy-start.3 = (f32[2,16,64,8]{3,2,1,0:T(8,128)S(1)}, f32[2,16,64,8]{3,2,1,0:T(8,128)}, u32[]{:S(2)}) copy-start(f32[2,16,64,8]{3,2,1,0:T(8,128)} %copy.47) | copy-start | bytes 196612
  89.5 22.9 %collective-permute-start.2 = (f32[2,16,8,272]{3,2,1,0:T(8,128)S(1)}, f32[2,16,8,272]{3,2,1,0:T(8,128)S(1)}, u32[]{:S(2)}, u32[]{:S(2)}) collective-permute-start(f32[2,16,8,272]{3,2,1,0:T(8,128)S(1)} %get-tuple-element.50), channel_id=1, source_target_pairs={{0,16},{16,32},{32,48},{48,64},{64,80},{80,96},{96,112},{112,128},... | collective-permute-start | bytes 835592 | tf_op jit(solution)/shard_map/ppermute | solution.py:47
  91.5 21.0 %collective-permute-start.3 = (f32[2,16,8,272]{3,2,1,0:T(8,128)S(1)}, f32[2,16,8,272]{3,2,1,0:T(8,128)S(1)}, u32[]{:S(2)}, u32[]{:S(2)}) collective-permute-start(f32[2,16,8,272]{3,2,1,0:T(8,128)S(1)} %get-tuple-element.51), channel_id=1, source_target_pairs={{16,0},{32,16},{48,32},{64,48},{80,64},{96,80},{112,96},{128,112},... | collective-permute-start | bytes 835592 | tf_op jit(solution)/shard_map/ppermute | solution.py:48
  114.3 1.9 copy-start.2
  116.2 7.6 %copy-start.19 = (s32[2,3,1,1,1]{1,4,3,2,0:T(1,128)S(1)}, s32[2,3,1,1,1]{1,4,3,2,0:T(1,128)}, u32[]{:S(2)}) copy-start(s32[2,3,1,1,1]{1,4,3,2,0:T(1,128)} %param.36) | copy-start | bytes 76
  116.3 28.0 %collective-permute-start.4 = (f32[9,80,272]{2,1,0:T(8,128)S(1)}, f32[9,80,272]{2,1,0:T(8,128)S(1)}, u32[]{:S(2)}, u32[]{:S(2)}) collective-permute-start(f32[9,80,272]{2,1,0:T(8,128)S(1)} %pad_maximum_fusion.6), channel_id=1, source_target_pairs={{1,0},{2,1},{3,2},{5,4},{6,5},{7,6},{9,8},{10,9},{11,10},{13,12},{... | collective-permute-start | bytes 2350088 | tf_op jit(solution)/shard_map/ppermute | solution.py:166
  118.7 28.8 %collective-permute-start.5 = (f32[9,80,272]{2,1,0:T(8,128)}, f32[9,80,272]{2,1,0:T(8,128)S(1)}, u32[]{:S(2)}, u32[]{:S(2)}) collective-permute-start(f32[9,80,272]{2,1,0:T(8,128)} %pad_maximum_fusion.7), channel_id=1, source_target_pairs={{0,1},{1,2},{2,3},{4,5},{5,6},{6,7},{8,9},{9,10},{10,11},{12,13},{... | collective-permute-start | bytes 2350088 | tf_op jit(solution)/shard_map/ppermute | solution.py:165
  131.4 24.8 %copy-start = (f32[16,80,272]{2,1,0:T(8,128)}, f32[16,80,272]{2,1,0:T(8,128)S(1)}, u32[]{:S(2)}) copy-start(f32[16,80,272]{2,1,0:T(8,128)S(1)} %get-tuple-element.53) | copy-start | bytes 4177924
  144.4 3.1 copy-start.7
  154.0 1.2 slice-start
  154.0 1.5 slice-start.1
  155.8 1.9 copy-start.4
  156.2 1.5 copy-start.16
  156.2 1.5 copy-start.17
  157.7 1.1 copy-start.6
  161.8 37.7 %copy-start.22 = (f32[6]{0:T(128)S(1)}, f32[6]{0:T(128)}, u32[]{:S(2)}) copy-start(f32[6]{0:T(128)} %constant.84) | copy-start | bytes 76
  162.2 6.6 %collective-permute-start.6 = (f32[9,1,9,33]{3,2,1,0:T(8,128)S(1)}, f32[9,1,9,33]{3,2,1,0:T(8,128)S(1)}, u32[]{:S(2)}, u32[]{:S(2)}) collective-permute-start(f32[9,1,9,33]{3,2,1,0:T(8,128)S(1)} %fusion.61), channel_id=1, source_target_pairs={{0,1},{1,2},{2,3},{4,5},{5,6},{6,7},{8,9},{9,10},{10,11},{12,13},{... | collective-permute-start | bytes 32084 | tf_op jit(solution)/shard_map/ppermute | solution.py:59
  168.9 6.7 %collective-permute-start.7 = (f32[9,1,9,33]{3,2,1,0:T(8,128)S(1)}, f32[9,1,9,33]{3,2,1,0:T(8,128)S(1)}, u32[]{:S(2)}, u32[]{:S(2)}) collective-permute-start(f32[9,1,9,33]{3,2,1,0:T(8,128)S(1)} %get-tuple-element.42), channel_id=1, source_target_pairs={{1,0},{2,1},{3,2},{5,4},{6,5},{7,6},{9,8},{10,9},{11,10},{13,12},{... | collective-permute-start | bytes 32084 | tf_op jit(solution)/shard_map/ppermute | solution.py:60
  175.6 10.4 %collective-permute-start.8 = (f32[9,3,1,33]{3,2,1,0:T(1,128)S(1)}, f32[9,3,1,33]{3,2,1,0:T(1,128)S(1)}, u32[]{:S(2)}, u32[]{:S(2)}) collective-permute-start(f32[9,3,1,33]{3,2,1,0:T(1,128)S(1)} %get-tuple-element.118), channel_id=1, source_target_pairs={{0,16},{16,32},{32,48},{48,64},{64,80},{80,96},{96,112},{112,128},... | collective-permute-start | bytes 10700 | tf_op jit(solution)/shard_map/ppermute | solution.py:59
  177.6 9.9 %collective-permute-start.9 = (f32[9,3,1,33]{3,2,1,0:T(1,128)S(1)}, f32[9,3,1,33]{3,2,1,0:T(1,128)S(1)}, u32[]{:S(2)}, u32[]{:S(2)}) collective-permute-start(f32[9,3,1,33]{3,2,1,0:T(1,128)S(1)} %get-tuple-element.119), channel_id=1, source_target_pairs={{16,0},{32,16},{48,32},{64,48},{80,64},{96,80},{112,96},{128,112},... | collective-permute-start | bytes 10700 | tf_op jit(solution)/shard_map/ppermute | solution.py:60
  187.6 7.5 %collective-permute-start.10 = (f32[9,3,9,1]{3,2,1,0:T(8,128)S(1)}, f32[9,3,9,1]{3,2,1,0:T(8,128)S(1)}, u32[]{:S(2)}, u32[]{:S(2)}) collective-permute-start(f32[9,3,9,1]{3,2,1,0:T(8,128)S(1)} %get-tuple-element.114), channel_id=1, source_target_pairs={{0,4},{4,8},{8,12},{1,5},{5,9},{9,13},{2,6},{6,10},{10,14},{3,7},{... | collective-permute-start | bytes 2924 | tf_op jit(solution)/shard_map/ppermute | solution.py:59
  190.5 8.7 %collective-permute-start.11 = (f32[9,3,9,1]{3,2,1,0:T(8,128)S(1)}, f32[9,3,9,1]{3,2,1,0:T(8,128)S(1)}, u32[]{:S(2)}, u32[]{:S(2)}) collective-permute-start(f32[9,3,9,1]{3,2,1,0:T(8,128)S(1)} %get-tuple-element.115), channel_id=1, source_target_pairs={{4,0},{8,4},{12,8},{5,1},{9,5},{13,9},{6,2},{10,6},{14,10},{7,3},{... | collective-permute-start | bytes 2924 | tf_op jit(solution)/shard_map/ppermute | solution.py:60
  203.0 5.4 %collective-permute-start.12 = (f32[3,1,9,33]{3,2,1,0:T(8,128)S(1)}, f32[3,1,9,33]{3,2,1,0:T(8,128)S(1)}, u32[]{:S(2)}, u32[]{:S(2)}) collective-permute-start(f32[3,1,9,33]{3,2,1,0:T(8,128)S(1)} %get-tuple-element.164), channel_id=1, source_target_pairs={{0,1},{1,2},{2,3},{4,5},{5,6},{6,7},{8,9},{9,10},{10,11},{12,13},{... | collective-permute-start | bytes 10700 | tf_op jit(solution)/shard_map/ppermute | solution.py:59
  206.9 5.7 %collective-permute-start.13 = (f32[3,1,9,33]{3,2,1,0:T(8,128)S(1)}, f32[3,1,9,33]{3,2,1,0:T(8,128)S(1)}, u32[]{:S(2)}, u32[]{:S(2)}) collective-permute-start(f32[3,1,9,33]{3,2,1,0:T(8,128)S(1)} %get-tuple-element.165), channel_id=1, source_target_pairs={{1,0},{2,1},{3,2},{5,4},{6,5},{7,6},{9,8},{10,9},{11,10},{13,12},{... | collective-permute-start | bytes 10700 | tf_op jit(solution)/shard_map/ppermute | solution.py:60
  212.6 9.7 %collective-permute-start.14 = (f32[3,3,1,33]{3,2,1,0:T(1,128)S(1)}, f32[3,3,1,33]{3,2,1,0:T(1,128)S(1)}, u32[]{:S(2)}, u32[]{:S(2)}) collective-permute-start(f32[3,3,1,33]{3,2,1,0:T(1,128)S(1)} %pad_maximum_fusion.32), channel_id=1, source_target_pairs={{0,16},{16,32},{32,48},{48,64},{64,80},{80,96},{96,112},{112,128},... | collective-permute-start | bytes 3572 | tf_op jit(solution)/shard_map/ppermute | solution.py:59
  222.4 3.2 collective-permute-start.15
  225.7 5.0 %collective-permute-start.16 = (f32[3,3,9,1]{3,2,1,0:T(8,128)S(1)}, f32[3,3,9,1]{3,2,1,0:T(8,128)S(1)}, u32[]{:S(2)}, u32[]{:S(2)}) collective-permute-start(f32[3,3,9,1]{3,2,1,0:T(8,128)S(1)} %get-tuple-element.159), channel_id=1, source_target_pairs={{0,4},{4,8},{8,12},{1,5},{5,9},{9,13},{2,6},{6,10},{10,14},{3,7},{... | collective-permute-start | bytes 980 | tf_op jit(solution)/shard_map/ppermute | solution.py:59
  228.8 6.2 %collective-permute-start.17 = (f32[3,3,9,1]{3,2,1,0:T(8,128)S(1)}, f32[3,3,9,1]{3,2,1,0:T(8,128)S(1)}, u32[]{:S(2)}, u32[]{:S(2)}) collective-permute-start(f32[3,3,9,1]{3,2,1,0:T(8,128)S(1)} %get-tuple-element.160), channel_id=1, source_target_pairs={{4,0},{8,4},{12,8},{5,1},{9,5},{13,9},{6,2},{10,6},{14,10},{7,3},{... | collective-permute-start | bytes 980 | tf_op jit(solution)/shard_map/ppermute | solution.py:60
  239.3 5.0 %collective-permute-start.18 = (f32[3,1,9,33]{3,2,1,0:T(8,128)S(1)}, f32[3,1,9,33]{3,2,1,0:T(8,128)S(1)}, u32[]{:S(2)}, u32[]{:S(2)}) collective-permute-start(f32[3,1,9,33]{3,2,1,0:T(8,128)S(1)} %get-tuple-element.155), channel_id=1, source_target_pairs={{0,1},{1,2},{2,3},{4,5},{5,6},{6,7},{8,9},{9,10},{10,11},{12,13},{... | collective-permute-start | bytes 10700 | tf_op jit(solution)/shard_map/ppermute | solution.py:59
  242.8 5.7 %collective-permute-start.19 = (f32[3,1,9,33]{3,2,1,0:T(8,128)S(1)}, f32[3,1,9,33]{3,2,1,0:T(8,128)S(1)}, u32[]{:S(2)}, u32[]{:S(2)}) collective-permute-start(f32[3,1,9,33]{3,2,1,0:T(8,128)S(1)} %get-tuple-element.156), channel_id=1, source_target_pairs={{1,0},{2,1},{3,2},{5,4},{6,5},{7,6},{9,8},{10,9},{11,10},{13,12},{... | collective-permute-start | bytes 10700 | tf_op jit(solution)/shard_map/ppermute | solution.py:60
  248.6 9.8 %copy-start.13 = (f32[3,1,9,33]{3,2,1,0:T(8,128)}, f32[3,1,9,33]{3,2,1,0:T(8,128)S(1)}, u32[]{:S(2)}) copy-start(f32[3,1,9,33]{3,2,1,0:T(8,128)S(1)} %get-tuple-element.152) | copy-start | bytes 10696
  248.6 9.8 %copy-start.14 = (f32[3,1,9,33]{3,2,1,0:T(8,128)}, f32[3,1,9,33]{3,2,1,0:T(8,128)S(1)}, u32[]{:S(2)}) copy-start(f32[3,1,9,33]{3,2,1,0:T(8,128)S(1)} %get-tuple-element.153) | copy-start | bytes 10696
  248.6 9.8 %copy-start.15 = (f32[3,1,9,33]{3,2,1,0:T(8,128)}, f32[3,1,9,33]{3,2,1,0:T(8,128)S(1)}, u32[]{:S(2)}) copy-start(f32[3,1,9,33]{3,2,1,0:T(8,128)S(1)} %get-tuple-element.154) | copy-start | bytes 10696
  248.6 9.7 %collective-permute-start.20 = (f32[3,3,1,33]{3,2,1,0:T(1,128)S(1)}, f32[3,3,1,33]{3,2,1,0:T(1,128)S(1)}, u32[]{:S(2)}, u32[]{:S(2)}) collective-permute-start(f32[3,3,1,33]{3,2,1,0:T(1,128)S(1)} %pad_maximum_fusion.30), channel_id=1, source_target_pairs={{0,16},{16,32},{32,48},{48,64},{64,80},{80,96},{96,112},{112,128},... | collective-permute-start | bytes 3572 | tf_op jit(solution)/shard_map/ppermute | solution.py:59
  258.4 5.6 %collective-permute-start.21 = (f32[3,3,1,33]{3,2,1,0:T(1,128)S(1)}, f32[3,3,1,33]{3,2,1,0:T(1,128)S(1)}, u32[]{:S(2)}, u32[]{:S(2)}) collective-permute-start(f32[3,3,1,33]{3,2,1,0:T(1,128)S(1)} %get-tuple-element.29), channel_id=1, source_target_pairs={{16,0},{32,16},{48,32},{64,48},{80,64},{96,80},{112,96},{128,112},... | collective-permute-start | bytes 3572 | tf_op jit(solution)/shard_map/ppermute | solution.py:60
  265.5 4.6 %collective-permute-start.22 = (f32[3,3,9,1]{3,2,1,0:T(8,128)}, f32[3,3,9,1]{3,2,1,0:T(8,128)}, u32[]{:S(2)}, u32[]{:S(2)}) collective-permute-start(f32[3,3,9,1]{3,2,1,0:T(8,128)} %get-tuple-element.150), channel_id=1, source_target_pairs={{0,4},{4,8},{8,12},{1,5},{5,9},{9,13},{2,6},{6,10},{10,14},{3,7},{... | collective-permute-start | bytes 980 | tf_op jit(solution)/shard_map/ppermute | solution.py:59
  268.3 6.6 %collective-permute-start.23 = (f32[3,3,9,1]{3,2,1,0:T(8,128)}, f32[3,3,9,1]{3,2,1,0:T(8,128)}, u32[]{:S(2)}, u32[]{:S(2)}) collective-permute-start(f32[3,3,9,1]{3,2,1,0:T(8,128)} %get-tuple-element.151), channel_id=1, source_target_pairs={{4,0},{8,4},{12,8},{5,1},{9,5},{13,9},{6,2},{10,6},{14,10},{7,3},{... | collective-permute-start | bytes 980 | tf_op jit(solution)/shard_map/ppermute | solution.py:60
  278.6 1.8 copy-start.1
  278.6 2.7 copy-start.5
  283.3 3.5 collective-permute-start.24
  285.3 5.7 %collective-permute-start.25 = (f32[3,1,9,33]{3,2,1,0:T(8,128)S(1)}, f32[3,1,9,33]{3,2,1,0:T(8,128)S(1)}, u32[]{:S(2)}, u32[]{:S(2)}) collective-permute-start(f32[3,1,9,33]{3,2,1,0:T(8,128)S(1)} %get-tuple-element.147), channel_id=1, source_target_pairs={{1,0},{2,1},{3,2},{5,4},{6,5},{7,6},{9,8},{10,9},{11,10},{13,12},{... | collective-permute-start | bytes 10700 | tf_op jit(solution)/shard_map/ppermute | solution.py:60
  291.1 9.7 %collective-permute-start.26 = (f32[3,3,1,33]{3,2,1,0:T(1,128)S(1)}, f32[3,3,1,33]{3,2,1,0:T(1,128)S(1)}, u32[]{:S(2)}, u32[]{:S(2)}) collective-permute-start(f32[3,3,1,33]{3,2,1,0:T(1,128)S(1)} %pad_maximum_fusion.28), channel_id=1, source_target_pairs={{0,16},{16,32},{32,48},{48,64},{64,80},{80,96},{96,112},{112,128},... | collective-permute-start | bytes 3572 | tf_op jit(solution)/shard_map/ppermute | solution.py:59
  300.8 3.2 collective-permute-start.27
  304.2 3.5 collective-permute-start.28
  305.7 6.2 %collective-permute-start.29 = (f32[3,3,9,1]{3,2,1,0:T(8,128)S(1)}, f32[3,3,9,1]{3,2,1,0:T(8,128)S(1)}, u32[]{:S(2)}, u32[]{:S(2)}) collective-permute-start(f32[3,3,9,1]{3,2,1,0:T(8,128)S(1)} %get-tuple-element.142), channel_id=1, source_target_pairs={{4,0},{8,4},{12,8},{5,1},{9,5},{13,9},{6,2},{10,6},{14,10},{7,3},{... | collective-permute-start | bytes 980 | tf_op jit(solution)/shard_map/ppermute | solution.py:60
  315.3 3.4 collective-permute-start.30
  317.2 5.7 %collective-permute-start.31 = (f32[3,1,9,33]{3,2,1,0:T(8,128)S(1)}, f32[3,1,9,33]{3,2,1,0:T(8,128)S(1)}, u32[]{:S(2)}, u32[]{:S(2)}) collective-permute-start(f32[3,1,9,33]{3,2,1,0:T(8,128)S(1)} %get-tuple-element.138), channel_id=1, source_target_pairs={{1,0},{2,1},{3,2},{5,4},{6,5},{7,6},{9,8},{10,9},{11,10},{13,12},{... | collective-permute-start | bytes 10700 | tf_op jit(solution)/shard_map/ppermute | solution.py:60
  323.0 9.7 %collective-permute-start.32 = (f32[3,3,1,33]{3,2,1,0:T(1,128)S(1)}, f32[3,3,1,33]{3,2,1,0:T(1,128)S(1)}, u32[]{:S(2)}, u32[]{:S(2)}) collective-permute-start(f32[3,3,1,33]{3,2,1,0:T(1,128)S(1)} %pad_maximum_fusion.26), channel_id=1, source_target_pairs={{0,16},{16,32},{32,48},{48,64},{64,80},{80,96},{96,112},{112,128},... | collective-permute-start | bytes 3572 | tf_op jit(solution)/shard_map/ppermute | solution.py:59
  332.7 3.2 collective-permute-start.33
  336.1 3.9 %collective-permute-start.34 = (f32[3,3,9,1]{3,2,1,0:T(8,128)S(1)}, f32[3,3,9,1]{3,2,1,0:T(8,128)S(1)}, u32[]{:S(2)}, u32[]{:S(2)}) collective-permute-start(f32[3,3,9,1]{3,2,1,0:T(8,128)S(1)} %get-tuple-element.132), channel_id=1, source_target_pairs={{0,4},{4,8},{8,12},{1,5},{5,9},{9,13},{2,6},{6,10},{10,14},{3,7},{... | collective-permute-start | bytes 980 | tf_op jit(solution)/shard_map/ppermute | solution.py:59
  338.0 6.2 %collective-permute-start.35 = (f32[3,3,9,1]{3,2,1,0:T(8,128)S(1)}, f32[3,3,9,1]{3,2,1,0:T(8,128)S(1)}, u32[]{:S(2)}, u32[]{:S(2)}) collective-permute-start(f32[3,3,9,1]{3,2,1,0:T(8,128)S(1)} %get-tuple-element.133), channel_id=1, source_target_pairs={{4,0},{8,4},{12,8},{5,1},{9,5},{13,9},{6,2},{10,6},{14,10},{7,3},{... | collective-permute-start | bytes 980 | tf_op jit(solution)/shard_map/ppermute | solution.py:60
  346.8 30.0 %copy-start.12 = (f32[1,3,9,33]{3,2,1,0:T(8,128)S(1)}, f32[1,3,9,33]{3,2,1,0:T(8,128)}, u32[]{:S(2)}) copy-start(f32[1,3,9,33]{3,2,1,0:T(8,128)} %copy-done.11) | copy-start | bytes 10696
  347.3 31.3 %copy-start.21 = (f32[3]{0:T(128)S(1)}, f32[3]{0:T(128)}, u32[]{:S(2)}) copy-start(f32[3]{0:T(128)} %get-tuple-element.173) | copy-start | bytes 40
  347.6 3.4 collective-permute-start.36
  349.5 5.7 %collective-permute-start.37 = (f32[3,1,9,33]{3,2,1,0:T(8,128)S(1)}, f32[3,1,9,33]{3,2,1,0:T(8,128)S(1)}, u32[]{:S(2)}, u32[]{:S(2)}) collective-permute-start(f32[3,1,9,33]{3,2,1,0:T(8,128)S(1)} %get-tuple-element.129), channel_id=1, source_target_pairs={{1,0},{2,1},{3,2},{5,4},{6,5},{7,6},{9,8},{10,9},{11,10},{13,12},{... | collective-permute-start | bytes 10700 | tf_op jit(solution)/shard_map/ppermute | solution.py:60
  355.3 9.7 %collective-permute-start.38 = (f32[3,3,1,33]{3,2,1,0:T(1,128)S(1)}, f32[3,3,1,33]{3,2,1,0:T(1,128)S(1)}, u32[]{:S(2)}, u32[]{:S(2)}) collective-permute-start(f32[3,3,1,33]{3,2,1,0:T(1,128)S(1)} %pad_maximum_fusion.24), channel_id=1, source_target_pairs={{0,16},{16,32},{32,48},{48,64},{64,80},{80,96},{96,112},{112,128},... | collective-permute-start | bytes 3572 | tf_op jit(solution)/shard_map/ppermute | solution.py:59
  365.0 3.2 collective-permute-start.39
  368.4 3.9 %collective-permute-start.40 = (f32[3,3,9,1]{3,2,1,0:T(8,128)S(1)}, f32[3,3,9,1]{3,2,1,0:T(8,128)S(1)}, u32[]{:S(2)}, u32[]{:S(2)}) collective-permute-start(f32[3,3,9,1]{3,2,1,0:T(8,128)S(1)} %get-tuple-element.123), channel_id=1, source_target_pairs={{0,4},{4,8},{8,12},{1,5},{5,9},{9,13},{2,6},{6,10},{10,14},{3,7},{... | collective-permute-start | bytes 980 | tf_op jit(solution)/shard_map/ppermute | solution.py:59
  370.3 6.2 %collective-permute-start.41 = (f32[3,3,9,1]{3,2,1,0:T(8,128)S(1)}, f32[3,3,9,1]{3,2,1,0:T(8,128)S(1)}, u32[]{:S(2)}, u32[]{:S(2)}) collective-permute-start(f32[3,3,9,1]{3,2,1,0:T(8,128)S(1)} %get-tuple-element.124), channel_id=1, source_target_pairs={{4,0},{8,4},{12,8},{5,1},{9,5},{13,9},{6,2},{10,6},{14,10},{7,3},{... | collective-permute-start | bytes 980 | tf_op jit(solution)/shard_map/ppermute | solution.py:60
  (7 other events, 5.6 us)
